TPU v7x, 128 devices: a whole 4x4x4 slice. The times are simulated.
128 devices in a mesh: half: 2 (over y_hi), tile: 64 (over x, y_lo, z, core).
Axes of the slice: x: 4, y: 4 (y_hi: 2, y_lo: 2; y = y_hi * 2 + y_lo), z: 4, core: 2. Of those that a mesh axis runs over, the one named last changes fastest.
Arguments:
- innov: bfloat16 [2, 1048576, 128], P('half', 'tile'), may hold values from -6 to 6
- pred: bfloat16 [2, 1048576, 128], P('half', 'tile'), may hold values from -0.59765625 to 0.59765625
- obs_weight: float32 [1048576], P('tile'), may hold values from 0.4 to 4
- owner: int32 [8192, 1], P('tile'), may hold values from 0 to 63; in each aligned block of 128 rows (0 to 127, 128 to 255, ...) at most 4 rows name the same one
- counts: int32 [64], P('tile'), may hold values from 64 to 128
- neighbours: int32 [64, 9], P('tile'), may hold values from 0 to 63, as said below
- loc_weight: float32 [64, 9], P('tile'), may hold values from 0.3 to 1
- ensemble: bfloat16 [2, 1048576, 128], P('half', 'tile'), may hold values from -6 to 6
Outputs:
- analysis: bfloat16 [2, 1048576, 128], P('half', 'tile')
Inputs may be any that keep to these rules, and one draw needn't show every extreme that they name: Of the 128 blocks of one tile at most 4 have the same owner, and some tile gives exactly 4 blocks to one owner; every tile owns some block. `neighbours`: each row names 9 different tiles, the first one being the row's own tile.
All inputs are finite; a program needn't handle non-finite values.
Results may differ from a plain program's by a relative error of at most 0.0072.
Values may be sent and summed in bfloat16 or wider, within the bound.
No kernel may reach another device: no remote copies, remote signals or barrier semaphores. Data moves between devices by JAX's collectives and lax.ppermute only.
A program may use at most 128 MiB of HBM per device.

v0:
```python
import jax
import jax.numpy as jnp
from jax import lax
from jax.sharding import PartitionSpec as P


def from_partner(block, axis, apart):
    count = lax.axis_size(axis)
    route = []
    for low in range(count):
        high = low | 1 << apart
        if high != low and high < count:
            route += [(low, high), (high, low)]
    return lax.ppermute(block, axis, route)


def per_device(innov, pred, obs_weight, owner, counts, neighbours, loc_weight, ensemble):
    tiles = lax.axis_size("tile")
    members = pred.shape[2]
    obs_rows = pred.shape[1]
    blocks = owner.shape[0]
    block_rows = obs_rows // blocks
    slot_count = max(2, 2 * blocks // tiles)
    block_ids = jnp.arange(blocks, dtype=jnp.int32)
    live = (block_ids < counts[0]).astype(jnp.float32)
    row_scale = obs_weight * jnp.repeat(live, block_rows)
    zed = (pred[0].astype(jnp.float32) * row_scale[:, None]).astype(jnp.bfloat16)
    unn = (innov[0].astype(jnp.float32) * row_scale[:, None]).astype(jnp.bfloat16)
    partner = from_partner(unn, "half", 0)
    dest = owner[:, 0]
    zed_b = zed.reshape(blocks, block_rows, members)
    partner_b = partner.reshape(blocks, block_rows, members)
    same = (dest[None, :] == dest[:, None]) & (block_ids[None, :] < block_ids[:, None])
    rank = jnp.sum(same.astype(jnp.int32), axis=1)
    position = dest * slot_count + rank
    slot_ids = jnp.arange(tiles * slot_count, dtype=jnp.int32)
    hit = position[None, :] == slot_ids[:, None]
    source = jnp.sum(hit.astype(jnp.int32) * block_ids[None, :], axis=1)
    filled = jnp.any(hit, axis=1)
    send_zed = jnp.where(filled[:, None, None], zed_b[source], jnp.zeros((), jnp.bfloat16))
    send_unn = jnp.where(filled[:, None, None], partner_b[source], jnp.zeros((), jnp.bfloat16))
    got_zed, got_unn = (
        lax.all_to_all(send_zed, "tile", split_axis=0, concat_axis=0, tiled=True),
        lax.all_to_all(send_unn, "tile", split_axis=0, concat_axis=0, tiled=True),
    )
    flat_zed = got_zed.reshape(-1, members)
    flat_unn = got_unn.reshape(-1, members)
    dims = (((0,), (0,)), ((), ()))
    gram = lax.dot_general(flat_zed, flat_zed, dims, preferred_element_type=jnp.float32)
    cross = lax.dot_general(flat_zed, flat_unn, dims, preferred_element_type=jnp.float32)
    eye = jnp.eye(members, dtype=jnp.float32)
    factor = jnp.linalg.cholesky((members - 1.0) * eye + gram)
    weights = jax.scipy.linalg.cho_solve((factor, True), cross)
    tile_ids = jnp.arange(tiles, dtype=jnp.int32)
    loc_row = jnp.sum(
        loc_weight[0][:, None] * (neighbours[0][:, None] == tile_ids[None, :]).astype(jnp.float32),
        axis=0,
    )
    spread = lax.psum_scatter(
        loc_row[:, None, None] * weights[None, :, :], "tile", scatter_dimension=0, tiled=True
    )[0].astype(jnp.bfloat16)
    ens_f = ensemble[0].astype(jnp.float32)
    center = jnp.mean(ens_f, axis=1, keepdims=True)
    anomalies = (ens_f - center).astype(jnp.bfloat16)
    made = jnp.dot(anomalies, spread, preferred_element_type=jnp.float32).astype(jnp.bfloat16)
    incr = from_partner(made, "half", 0)
    analysis = (ens_f + incr.astype(jnp.float32)).astype(jnp.bfloat16)
    return analysis[None]


def solution(mesh):
    return jax.shard_map(
        per_device,
        mesh=mesh,
        in_specs=(
            P("half", "tile", None),
            P("half", "tile", None),
            P("tile"),
            P("tile", None),
            P("tile"),
            P("tile", None),
            P("tile", None),
            P("half", "tile", None),
        ),
        out_specs=P("half", "tile", None),
        check_vma=False,
    )
```

profile of v0, /device:TPU:0, one launch (start us, length us, event | category | flops | bytes accessed | tf_op | source)
XLA Modules:
  0.0 763.2 jit_solution(8902518556873263066)
XLA Ops:
  7.4 1.3 bitcast_multiply_fusion
  8.7 5.8 fusion.3
  14.5 3.3 collective-permute-start
  17.8 0.2 convert_reduce_fusion.1
  18.0 0.1 select_reduce_fusion
  18.2 4.4 fusion.4
  22.6 10.6 %gather_fusion = bf16[256,128,128]{2,1,0:T(8,128)(2,1)} fusion(bf16[128,128,128]{2,1,0:T(8,128)(2,1)} %fusion.4, s32[1024]{0:T(1024)S(1)} %pad_clamp_fusion), kind=kCustom, calls=%fused_computation | custom fusion | bytes 16778240 | tf_op jit(solution)/shard_map/gather | solution.py:40
  33.2 0.1 fusion.9
  33.3 75.4 %collective-permute-done = bf16[16384,128]{1,0:T(8,128)(2,1)} collective-permute-done((bf16[16384,128]{1,0:T(8,128)(2,1)}, bf16[16384,128]{1,0:T(8,128)(2,1)}, u32[]{:S(2)}, u32[]{:S(2)}) %collective-permute-start) | collective-permute-done | bytes 4194336 | tf_op jit(solution)/shard_map/ppermute | solution.py:14
  108.7 10.6 %gather_fusion.1 = bf16[256,128,128]{2,1,0:T(8,128)(2,1)} fusion(bf16[128,128,128]{2,1,0:T(8,128)(2,1)} %bitcast.16, s32[1024]{0:T(1024)S(1)} %pad_clamp_fusion), kind=kCustom, calls=%fused_computation.1 | custom fusion | bytes 16778240 | tf_op jit(solution)/shard_map/gather | solution.py:41
  119.3 9.4 %broadcast_select_fusion = (bf16[256,128,128]{2,1,0:T(8,128)(2,1)}, bf16[256,128,128]{2,1,0:T(8,128)(2,1)S(1)}) fusion(bf16[256,128,128]{2,1,0:T(8,128)(2,1)} %gather_fusion.1, pred[256]{0:T(512)(128)(4,1)S(1)} %fusion.9, bf16[256,128,128]{2,1,0:T(8,128)(2,1)} %gather_fusion), kind=kLoop, calls=%fused_computation.13 | loop fusion | flops 8388608 | bytes 33554688 | tf_op jit(solution)/shard_map/jit(_where)/select_n | solution.py:41
  128.8 105.7 %all_to_all.10 = bf16[256,128,128]{2,1,0:T(8,128)(2,1)} all-to-all(bf16[256,128,128]{2,1,0:T(8,128)(2,1)S(1)} %get-tuple-element.6), channel_id=1, replica_groups=mesh['half'=2,'tile'=64] {'tile'}, dimensions={0} | all-to-all | bytes 16777216 | tf_op jit(solution)/shard_map/all_to_all | solution.py:43
  234.5 7.4 all-to-all-start.1
  241.9 0.2 reduce-scatter.2.cloned.1.call-start
  242.2 0.1 select_reduce_fusion.2
  242.2 8.2 %convolution_bitcast_fusion.1 = f32[128,128]{1,0:T(8,128)S(1)} fusion(bf16[256,128,128]{2,1,0:T(8,128)(2,1)} %all_to_all.10), kind=kOutput, calls=%fused_computation.20 | convolution fusion | flops 1073741824 | bytes 8454144 | tf_op jit(solution)/shard_map/dot_general | solution.py:49
  250.4 0.1 copy.14
  250.5 11.7 %cholesky.16 = f32[128,128]{1,0:T(8,128)S(1)} custom-call(f32[128,128]{1,0:T(8,128)S(1)} %fusion.16), custom_call_target="Cholesky" | custom-call | tf_op jit(solution)/shard_map/jit(cholesky)/cholesky | solution.py:52
  262.3 0.6 compare_reduce_fusion
  262.9 0.7 fusion.10
  263.6 9.8 %custom-call.10 = f32[1,128,128]{1,2,0:T(8,128)S(1)} custom-call(f32[1,128,128]{2,1,0:T(8,128)S(1)} %fusion.10), custom_call_target="InvertDiagBlocksLowerTriangular" | custom-call | tf_op jit(solution)/shard_map/jit(_cho_solve)/triangular_solve | solution.py:53
  273.4 75.6 %all-to-all-done.1 = bf16[256,128,128]{2,1,0:T(8,128)(2,1)} async-done(((bf16[256,128,128]{2,1,0:T(8,128)(2,1)}), bf16[256,128,128]{2,1,0:T(8,128)(2,1)}, u32[]{:S(2)}, u32[]{:S(2)}) %all-to-all-start.1) | async-done | bytes 8388640 | tf_op jit(solution)/shard_map/all_to_all | solution.py:44
  349.0 8.2 %convolution_bitcast_fusion = f32[128,128]{1,0:T(8,128)S(1)} fusion(bf16[256,128,128]{2,1,0:T(8,128)(2,1)} %all_to_all.10, bf16[256,128,128]{2,1,0:T(8,128)(2,1)} %all-to-all-done.1), kind=kOutput, calls=%fused_computation.19 | convolution fusion | flops 1073741824 | bytes 16842752 | tf_op jit(solution)/shard_map/dot_general | solution.py:50
  357.2 0.3 fusion.13
  357.4 0.2 fusion.11
  357.7 2.4 broadcast_multiply_fusion
  360.0 3.1 convert_reduce_fusion
  363.1 294.1 %reduce-scatter.2.cloned.1.call-done = f32[1,128,128]{2,1,0:T(8,128)} async-done(((f32[64,128,128]{2,1,0:T(8,128)}), f32[1,128,128]{2,1,0:T(8,128)}) %reduce-scatter.2.cloned.1.call-update) | async-done | bytes 65552 | tf_op jit(solution)/shard_map/reduce_scatter | solution.py:59
  657.3 8.6 %convolution_convert_fusion = bf16[16384,128]{1,0:T(8,128)(2,1)S(1)} fusion(bf16[1,16384,128]{2,1,0:T(8,128)(2,1)} %param.15, f32[16384]{0:T(1024)S(1)} %broadcast_multiply_fusion.1, f32[1,128,128]{2,1,0:T(8,128)} %reduce-scatter.2.cloned.1.call-done), kind=kOutput, calls=%fused_computation.2 | convolution fusion | flops 545275904 | bytes 8519680 | tf_op jit(solution)/shard_map/dot_general | solution.py:65
  665.9 2.8 collective-permute-start.1
  668.7 85.1 %collective-permute-done.1 = bf16[16384,128]{1,0:T(8,128)(2,1)S(1)} collective-permute-done((bf16[16384,128]{1,0:T(8,128)(2,1)S(1)}, bf16[16384,128]{1,0:T(8,128)(2,1)S(1)}, u32[]{:S(2)}, u32[]{:S(2)}) %collective-permute-start.1) | collective-permute-done | bytes 4194336 | tf_op jit(solution)/shard_map/ppermute | solution.py:14
  753.8 2.6 fusion.7
  (18 shorter events, 0.1 us)
Async XLA Ops:
  6.5 11.3 %copy-start.2 = (s32[128,1]{0,1:T(1,128)S(1)}, s32[128,1]{0,1:T(1,128)}, u32[]{:S(2)}) copy-start(s32[128,1]{0,1:T(1,128)} %param.11) | copy-start | bytes 1540
  6.5 11.6 %copy-start.1 = (bf16[1,16384,128]{2,1,0:T(8,128)(2,1)S(1)}, bf16[1,16384,128]{2,1,0:T(8,128)(2,1)}, u32[]{:S(2)}) copy-start(bf16[1,16384,128]{2,1,0:T(8,128)(2,1)} %param.9) | copy-start | bytes 12582916
  14.5 94.2 %collective-permute-start = (bf16[16384,128]{1,0:T(8,128)(2,1)}, bf16[16384,128]{1,0:T(8,128)(2,1)}, u32[]{:S(2)}, u32[]{:S(2)}) collective-permute-start(bf16[16384,128]{1,0:T(8,128)(2,1)} %fusion.3), channel_id=1, source_target_pairs={{0,64},{64,0},{1,65},{65,1},{2,66},{66,2},{3,67},{67,3},{4,68},{68... | collective-permute-start | bytes 12582920 | tf_op jit(solution)/shard_map/ppermute | solution.py:14
  234.5 7.6 %copy-start.3 = (f32[1,9]{1,0:T(1,128)S(1)}, f32[1,9]{1,0:T(1,128)}, u32[]{:S(2)}) copy-start(f32[1,9]{1,0:T(1,128)} %param.14) | copy-start | bytes 112
  234.5 7.7 %copy-start.4 = (s32[1,9]{1,0:T(1,128)S(1)}, s32[1,9]{1,0:T(1,128)}, u32[]{:S(2)}) copy-start(s32[1,9]{1,0:T(1,128)} %param.13) | copy-start | bytes 112
  234.5 114.5 %all-to-all-start.1 = ((bf16[256,128,128]{2,1,0:T(8,128)(2,1)}), bf16[256,128,128]{2,1,0:T(8,128)(2,1)}, u32[]{:S(2)}, u32[]{:S(2)}) async-start(bf16[256,128,128]{2,1,0:T(8,128)(2,1)} %get-tuple-element.5), calls=%async_computation.1 | async-start | bytes 16777216 | tf_op jit(solution)/shard_map/all_to_all | solution.py:44
  241.9 415.4 %reduce-scatter.2.cloned.1.call-start = ((), (), s32[]{:S(2)}) async-start(), calls=%async_computation.3 | async-start | bytes 4259840 | tf_op jit(solution)/shard_map/reduce_scatter | solution.py:59
  657.3 96.5 %copy-start = (bf16[1,16384,128]{2,1,0:T(8,128)(2,1)S(1)}, bf16[1,16384,128]{2,1,0:T(8,128)(2,1)}, u32[]{:S(2)}) copy-start(bf16[1,16384,128]{2,1,0:T(8,128)(2,1)} %param.15) | copy-start | bytes 12582916
  665.9 87.9 %collective-permute-start.1 = (bf16[16384,128]{1,0:T(8,128)(2,1)S(1)}, bf16[16384,128]{1,0:T(8,128)(2,1)S(1)}, u32[]{:S(2)}, u32[]{:S(2)}) collective-permute-start(bf16[16384,128]{1,0:T(8,128)(2,1)S(1)} %convolution_convert_fusion), channel_id=1, source_target_pairs={{0,64},{64,0},{1,65},{65,1},{2,66},{66,2},{3,67},{67,3},{4,68},{68... | collective-permute-start | bytes 12582920 | tf_op jit(solution)/shard_map/ppermute | solution.py:14
Sparse Core Ops, SparseCore 0:
  360.2 297.0 reduce-scatter.1
where the time goes:
time: 764 us; the launch traced here: 763 us
  waiting for transfers between devices  530 us (69%)
  blocking collectives  106 us (14%)
  other arithmetic  52.4 us (7%)
  matrix products  25.4 us (3%)
  local copies, waits for them, and re-layouts  21.4 us (3%)
  between operations  14.4 us (2%)
  starting transfers between devices  13.7 us (2%)
    reduce_scatter x1, waiting for transfers between devices, per_device(): lax.psum_scatter(loc_row[:, None, None] * weights[None, :, :], 'tile', sc...  294 us
    ppermute x2, waiting for transfers between devices, from_partner(): return lax.ppermute(block, axis, route)  160 us
    all_to_all x1, blocking collectives, per_device(): lax.all_to_all(send_zed, 'tile', split_axis=0, concat_axis=0, tiled=True)  106 us
    all_to_all x1, waiting for transfers between devices, per_device(): lax.all_to_all(send_unn, 'tile', split_axis=0, concat_axis=0, tiled=True)  75.6 us
  transfers between devices with their start and end apart: 4, of which 4 were waited for; matrix products, arithmetic and copies ran while one was open for 7% of the time, Pallas kernels for 0%

commit v1 on v0

v1 whole, which is shorter than its diff:
```python
import jax
import jax.numpy as jnp
from jax import lax
from jax.sharding import PartitionSpec as P


def from_partner(block, axis, apart):
    count = lax.axis_size(axis)
    route = []
    for low in range(count):
        high = low | 1 << apart
        if high != low and high < count:
            route += [(low, high), (high, low)]
    return lax.ppermute(block, axis, route)


def step(innov, pred, obs_weight, owner, counts, neighbours, loc_weight, ensemble):
    tiles = lax.axis_size("tile")
    members = pred.shape[2]
    obs_rows = pred.shape[1]
    blocks = owner.shape[0]
    block_rows = obs_rows // blocks
    slot_count = max(2, 2 * blocks // tiles)
    block_ids = jnp.arange(blocks, dtype=jnp.int32)
    live = (block_ids < counts[0]).astype(jnp.float32)
    row_scale = obs_weight * jnp.repeat(live, block_rows)
    zed = (pred[0].astype(jnp.float32) * row_scale[:, None]).astype(jnp.bfloat16)
    unn = (innov[0].astype(jnp.float32) * row_scale[:, None]).astype(jnp.bfloat16)
    partner = from_partner(unn, "half", 0)
    ens_f = ensemble[0].astype(jnp.float32)
    center = jnp.mean(ens_f, axis=1, keepdims=True)
    anomalies = (ens_f - center).astype(jnp.bfloat16)
    anomalies, partner = lax.optimization_barrier((anomalies, partner))
    partner_anom = from_partner(anomalies, "half", 0)

    dest = owner[:, 0]
    zed_b = zed.reshape(blocks, block_rows, members)
    partner_b = partner.reshape(blocks, block_rows, members)
    same = (dest[None, :] == dest[:, None]) & (block_ids[None, :] < block_ids[:, None])
    rank = jnp.sum(same.astype(jnp.int32), axis=1)
    position = dest * slot_count + rank
    slot_ids = jnp.arange(tiles * slot_count, dtype=jnp.int32)
    hit = position[None, :] == slot_ids[:, None]
    source = jnp.sum(hit.astype(jnp.int32) * block_ids[None, :], axis=1)
    filled = jnp.any(hit, axis=1)
    slot_zed = jnp.where(filled[:, None, None], zed_b[source], jnp.zeros((), jnp.bfloat16))
    slot_zed = slot_zed.reshape(tiles, slot_count * block_rows, members)
    slot_unn = jnp.where(filled[:, None, None], partner_b[source], jnp.zeros((), jnp.bfloat16))
    slot_unn = slot_unn.reshape(tiles, slot_count * block_rows, members)
    dims = (((1,), (1,)), ((0,), (0,)))
    gram_part = lax.dot_general(slot_zed, slot_zed, dims, preferred_element_type=jnp.float32)
    gram_got = lax.all_to_all(gram_part, "tile", 0, 0, tiled=True)
    gram = jnp.sum(gram_got, axis=0)
    cross_part = lax.dot_general(slot_zed, slot_unn, dims, preferred_element_type=jnp.float32)
    cross = jnp.sum(lax.all_to_all(cross_part, "tile", 0, 0, tiled=True), axis=0)
    eye = jnp.eye(members, dtype=jnp.float32)
    factor = jnp.linalg.cholesky((members - 1.0) * eye + gram)
    weights = jax.scipy.linalg.cho_solve((factor, True), cross)
    tile_ids = jnp.arange(tiles, dtype=jnp.int32)
    loc_row = jnp.sum(
        loc_weight[0][:, None] * (neighbours[0][:, None] == tile_ids[None, :]).astype(jnp.float32),
        axis=0,
    )
    reach = loc_row[:, None, None] * weights[None, :, :]
    spread = jnp.sum(lax.all_to_all(reach, "tile", 0, 0, tiled=True), axis=0).astype(jnp.bfloat16)
    partner_spread = from_partner(spread, "half", 0)
    incr = jnp.dot(partner_anom, partner_spread, preferred_element_type=jnp.float32).astype(jnp.bfloat16)
    analysis = (ens_f + incr.astype(jnp.float32)).astype(jnp.bfloat16)
    return analysis[None]


def solution(mesh):
    return jax.shard_map(
        step,
        mesh=mesh,
        in_specs=(
            P("half", "tile", None),
            P("half", "tile", None),
            P("tile"),
            P("tile", None),
            P("tile"),
            P("tile", None),
            P("tile", None),
            P("half", "tile", None),
        ),
        out_specs=P("half", "tile", None),
        check_vma=False,
    )
```

time: 764 us -> 406 us (0.53)
  waiting for transfers between devices: 530 us -> 133 us
  blocking collectives: 106 us -> 130 us
  starting transfers between devices: 13.7 us -> 28 us
  between operations: 14.4 us -> 0.98 us
  other arithmetic: 52.4 us -> 62.8 us
    reduce_scatter x1 -> x0, waiting for transfers between devices: 294 us -> none  [per_device(): lax.psum_scatter(loc_row[:, None, None] * weights[None, :, :], 'tile', sc...]
    ppermute x2 -> x3, waiting for transfers between devices: 160 us -> 69.1 us  [from_partner(): return lax.ppermute(block, axis, route)]
    all_to_all x1, blocking collectives: 106 us -> 130 us  [step(): lax.all_to_all(reach, 'tile', 0, 0, tiled=True)]
    all_to_all x1 -> x2, waiting for transfers between devices: 75.6 us -> 63.8 us  [the longest x1 41 us: step(): gram_got = lax.all_to_all(gram_part, 'tile', 0, 0, tiled=True)]
    all_to_all x1 -> x2, starting transfers between devices: 7.4 us -> 18.7 us  [the longest x1 10.1 us: step(): gram_got = lax.all_to_all(gram_part, 'tile', 0, 0, tiled=True)]
    convert_element_type x3 -> x4, other arithmetic: 10.2 us -> 17.4 us  [the longest x1 5.82 us: step(): (innov[0].astype(jnp.float32) * row_scale[:, None]).astype(jnp.bfloat16)]
  transfers between devices with their start and end apart: 4 -> 5, of which waited for: 4 -> 4; matrix products, arithmetic and copies ran while one was open for 7% -> 16% of each run, Pallas kernels for 0% -> 0%
where the time goes in v1:
time: 406 us; the launch traced here: 404 us
  waiting for transfers between devices  133 us (33%)
  blocking collectives  130 us (32%)
  other arithmetic  62.8 us (15%)
  starting transfers between devices  28 us (7%)
  matrix products  27.5 us (7%)
  local copies, waits for them, and re-layouts  21.6 us (5%)
    all_to_all x1, blocking collectives, step(): lax.all_to_all(reach, 'tile', 0, 0, tiled=True)  130 us
    ppermute x3, waiting for transfers between devices, from_partner(): return lax.ppermute(block, axis, route)  69.1 us
    all_to_all x1, waiting for transfers between devices, step(): gram_got = lax.all_to_all(gram_part, 'tile', 0, 0, tiled=True)  41 us
    all_to_all x1, waiting for transfers between devices, step(): lax.all_to_all(cross_part, 'tile', 0, 0, tiled=True)  22.8 us
    another operation x3, other arithmetic, step(): factor = jnp.linalg.cholesky((members - 1.0) * eye + gram)  12.4 us
    select_n x1, other arithmetic, step(): jnp.where(filled[:, None, None], partner_b[source], jnp.zeros((), jnp.bfl...  11.9 us
    gather x1, local copies, waits for them, and re-layouts, step(): zed_b[source]  10.6 us
    gather x1, local copies, waits for them, and re-layouts, step(): partner_b[source]  10.6 us
  transfers between devices with their start and end apart: 5, of which 4 were waited for; matrix products, arithmetic and copies ran while one was open for 16% of the time, Pallas kernels for 0%

profile of v1, /device:TPU:0, one launch (start us, length us, event | category | flops | bytes accessed | tf_op | source)
XLA Modules:
  0.0 403.6 jit_solution(16709283882532308329)
XLA Ops:
  0.8 1.3 bitcast_multiply_fusion
  2.2 5.8 %fusion.7 = bf16[16384,128]{1,0:T(8,128)(2,1)} fusion(bf16[1,16384,128]{2,1,0:T(8,128)(2,1)} %param.8, f32[16384]{0:T(1024)S(1)} %bitcast_multiply_fusion), kind=kLoop, calls=%fused_computation.14 | loop fusion | flops 6291456 | bytes 8454144 | tf_op jit(solution)/shard_map/convert_element_type | solution.py:28
  8.0 3.3 collective-permute-start
  11.3 0.2 convert_reduce_fusion.1
  11.7 1.3 convert_reduce_fusion
  13.3 5.8 %fusion.6 = bf16[128,128,128]{2,1,0:T(8,128)(2,1)} fusion(bf16[128,128,128]{2,1,0:T(8,128)(2,1)} %bitcast.59, f32[128,128]{1,0:T(8,128)S(1)} %bitcast.60), kind=kLoop, calls=%fused_computation.12 | loop fusion | flops 6291456 | bytes 8454144 | tf_op jit(solution)/shard_map/convert_element_type | solution.py:27
  19.1 10.6 %gather_fusion = bf16[256,128,128]{2,1,0:T(8,128)(2,1)} fusion(bf16[128,128,128]{2,1,0:T(8,128)(2,1)} %fusion.6, s32[1024]{0:T(1024)S(1)} %pad_clamp_fusion), kind=kCustom, calls=%fused_computation | custom fusion | bytes 16778240 | tf_op jit(solution)/shard_map/gather | solution.py:46
  29.8 5.8 %fusion.5 = bf16[16384,128]{1,0:T(8,128)(2,1)} fusion(bf16[1,16384,128]{2,1,0:T(8,128)(2,1)} %param.15, f32[16384]{0:T(1024)S(1)} %broadcast_multiply_fusion.1), kind=kLoop, calls=%fused_computation.10 | loop fusion | flops 6291456 | bytes 8454144 | tf_op jit(solution)/shard_map/convert_element_type | solution.py:32
  35.6 66.6 %collective-permute-done = bf16[16384,128]{1,0:T(8,128)(2,1)} collective-permute-done((bf16[16384,128]{1,0:T(8,128)(2,1)}, bf16[16384,128]{1,0:T(8,128)(2,1)}, u32[]{:S(2)}, u32[]{:S(2)}) %collective-permute-start) | collective-permute-done | bytes 4194336 | tf_op jit(solution)/shard_map/ppermute | solution.py:14
  102.2 10.6 %gather_fusion.1 = bf16[256,128,128]{2,1,0:T(8,128)(2,1)} fusion(bf16[128,128,128]{2,1,0:T(8,128)(2,1)} %bitcast.15, s32[1024]{0:T(1024)S(1)} %pad_clamp_fusion), kind=kCustom, calls=%fused_computation.1 | custom fusion | bytes 16778240 | tf_op jit(solution)/shard_map/gather | solution.py:48
  112.8 11.9 %bitcast_select_fusion = (bf16[64,512,128]{2,1,0:T(8,128)(2,1)}, bf16[64,512,128]{2,1,0:T(8,128)(2,1)}) fusion(pred[64,512]{1,0:T(8,128)(4,1)S(1)} %bitcast.61, bf16[64,512,128]{2,1,0:T(8,128)(2,1)} %bitcast.58, bf16[64,512,128]{2,1,0:T(8,128)(2,1)} %bitcast.57), kind=kLoop, calls=%fused_computation.15 | loop fusion | flops 8388608 | bytes 33587200 | tf_op jit(solution)/shard_map/jit(_where)/select_n | solution.py:48
  124.7 10.2 %fusion.17 = f32[64,128,128]{2,1,0:T(8,128)} fusion(bf16[64,512,128]{2,1,0:T(8,128)(2,1)} %get-tuple-element.10), kind=kOutput, calls=%fused_computation.47 | convolution fusion | flops 1073741824 | bytes 12582912 | tf_op jit(solution)/shard_map/dot_general | solution.py:51
  134.9 10.1 %all-to-all-start = ((f32[64,128,128]{2,1,0:T(8,128)}), f32[64,128,128]{2,1,0:T(8,128)}, u32[]{:S(2)}, u32[]{:S(2)}) async-start(f32[64,128,128]{2,1,0:T(8,128)} %fusion.17), calls=%async_computation | async-start | bytes 8388608 | tf_op jit(solution)/shard_map/all_to_all | solution.py:52
  145.0 10.1 %fusion.18 = f32[64,128,128]{2,1,0:T(8,128)} fusion(bf16[64,512,128]{2,1,0:T(8,128)(2,1)} %get-tuple-element.10, bf16[64,512,128]{2,1,0:T(8,128)(2,1)} %get-tuple-element.9), kind=kOutput, calls=%fused_computation.48 | convolution fusion | flops 1073741824 | bytes 20971520 | tf_op jit(solution)/shard_map/dot_general | solution.py:54
  155.2 41.0 %all-to-all-done = f32[64,128,128]{2,1,0:T(8,128)} async-done(((f32[64,128,128]{2,1,0:T(8,128)}), f32[64,128,128]{2,1,0:T(8,128)}, u32[]{:S(2)}, u32[]{:S(2)}) %all-to-all-start) | async-done | bytes 4194336 | tf_op jit(solution)/shard_map/all_to_all | solution.py:52
  196.2 8.6 %all-to-all-start.1 = ((f32[64,128,128]{2,1,0:T(8,128)}), f32[64,128,128]{2,1,0:T(8,128)}, u32[]{:S(2)}, u32[]{:S(2)}) async-start(f32[64,128,128]{2,1,0:T(8,128)} %fusion.18), calls=%async_computation.1 | async-start | bytes 8388608 | tf_op jit(solution)/shard_map/all_to_all | solution.py:55
  204.9 3.0 collective-permute-start.1
  207.9 2.4 reduce_sum.72
  210.4 11.7 %cholesky.16 = f32[128,128]{1,0:T(8,128)S(1)} custom-call(f32[128,128]{1,0:T(8,128)S(1)} %fusion.15), custom_call_target="Cholesky" | custom-call | tf_op jit(solution)/shard_map/jit(cholesky)/cholesky | solution.py:57
  222.1 0.6 compare_reduce_fusion
  222.8 0.6 fusion.9
  223.3 9.8 %custom-call.10 = f32[1,128,128]{1,2,0:T(8,128)S(1)} custom-call(f32[1,128,128]{2,1,0:T(8,128)S(1)} %fusion.9), custom_call_target="InvertDiagBlocksLowerTriangular" | custom-call | tf_op jit(solution)/shard_map/jit(_cho_solve)/triangular_solve | solution.py:58
  233.2 22.8 %all-to-all-done.1 = f32[64,128,128]{2,1,0:T(8,128)} async-done(((f32[64,128,128]{2,1,0:T(8,128)}), f32[64,128,128]{2,1,0:T(8,128)}, u32[]{:S(2)}, u32[]{:S(2)}) %all-to-all-start.1) | async-done | bytes 4194336 | tf_op jit(solution)/shard_map/all_to_all | solution.py:55
  255.9 2.4 reduce_sum.74
  258.3 0.3 fusion.12
  258.6 0.2 fusion.10
  258.8 0.3 broadcast_multiply_fusion
  259.2 129.8 %all_to_all.15 = f32[64,128,128]{2,1,0:T(8,128)} all-to-all(f32[64,128,128]{2,1,0:T(8,128)S(1)} %broadcast_multiply_fusion), channel_id=1, replica_groups=mesh['half'=2,'tile'=64] {'tile'}, dimensions={0} | all-to-all | bytes 8388608 | tf_op jit(solution)/shard_map/all_to_all | solution.py:65
  389.0 2.4 reduce_sum.75
  391.4 3.0 collective-permute-start.2
  394.4 2.5 collective-permute-done.2
  396.9 6.7 %fusion.3 = bf16[1,16384,128]{2,1,0:T(8,128)(2,1)} fusion(bf16[16384,128]{1,0:T(8,128)(2,1)} %collective-permute-done.1, bf16[128,128]{1,0:T(8,128)(2,1)S(1)} %collective-permute-done.2, bf16[1,16384,128]{2,1,0:T(8,128)(2,1)} %param.15), kind=kOutput, calls=%fused_computation.6 | convolution fusion | flops 547356672 | bytes 12615680 | tf_op jit(solution)/shard_map/dot_general | solution.py:67
  (23 shorter events, 0.8 us)
Async XLA Ops:
  0.0 11.3 %copy-start.1 = (s32[128,1]{0,1:T(1,128)S(1)}, s32[128,1]{0,1:T(1,128)}, u32[]{:S(2)}) copy-start(s32[128,1]{0,1:T(1,128)} %param.11) | copy-start | bytes 1540
  0.0 11.7 %copy-start = (bf16[1,16384,128]{2,1,0:T(8,128)(2,1)S(1)}, bf16[1,16384,128]{2,1,0:T(8,128)(2,1)}, u32[]{:S(2)}) copy-start(bf16[1,16384,128]{2,1,0:T(8,128)(2,1)} %param.15) | copy-start | bytes 12582916
  8.0 94.2 %collective-permute-start = (bf16[16384,128]{1,0:T(8,128)(2,1)}, bf16[16384,128]{1,0:T(8,128)(2,1)}, u32[]{:S(2)}, u32[]{:S(2)}) collective-permute-start(bf16[16384,128]{1,0:T(8,128)(2,1)} %fusion.7), channel_id=1, source_target_pairs={{0,64},{64,0},{1,65},{65,1},{2,66},{66,2},{3,67},{67,3},{4,68},{68... | collective-permute-start | bytes 12582920 | tf_op jit(solution)/shard_map/ppermute | solution.py:14
  134.9 61.3 %all-to-all-start = ((f32[64,128,128]{2,1,0:T(8,128)}), f32[64,128,128]{2,1,0:T(8,128)}, u32[]{:S(2)}, u32[]{:S(2)}) async-start(f32[64,128,128]{2,1,0:T(8,128)} %fusion.17), calls=%async_computation | async-start | bytes 8388608 | tf_op jit(solution)/shard_map/all_to_all | solution.py:52
  155.1 49.6 %copy-start.2 = (f32[1,9]{1,0:T(1,128)S(1)}, f32[1,9]{1,0:T(1,128)}, u32[]{:S(2)}) copy-start(f32[1,9]{1,0:T(1,128)} %param.14) | copy-start | bytes 112
  155.2 49.6 %copy-start.3 = (s32[1,9]{1,0:T(1,128)S(1)}, s32[1,9]{1,0:T(1,128)}, u32[]{:S(2)}) copy-start(s32[1,9]{1,0:T(1,128)} %param.13) | copy-start | bytes 112
  196.2 59.7 %all-to-all-start.1 = ((f32[64,128,128]{2,1,0:T(8,128)}), f32[64,128,128]{2,1,0:T(8,128)}, u32[]{:S(2)}, u32[]{:S(2)}) async-start(f32[64,128,128]{2,1,0:T(8,128)} %fusion.18), calls=%async_computation.1 | async-start | bytes 8388608 | tf_op jit(solution)/shard_map/all_to_all | solution.py:55
  204.9 189.5 %collective-permute-start.1 = (bf16[16384,128]{1,0:T(8,128)(2,1)}, bf16[16384,128]{1,0:T(8,128)(2,1)}, u32[]{:S(2)}, u32[]{:S(2)}) collective-permute-start(bf16[16384,128]{1,0:T(8,128)(2,1)} %fusion.5), channel_id=1, source_target_pairs={{0,64},{64,0},{1,65},{65,1},{2,66},{66,2},{3,67},{67,3},{4,68},{68... | collective-permute-start | bytes 12582920 | tf_op jit(solution)/shard_map/ppermute | solution.py:14
  391.4 5.5 %collective-permute-start.2 = (bf16[128,128]{1,0:T(8,128)(2,1)S(1)}, bf16[128,128]{1,0:T(8,128)(2,1)S(1)}, u32[]{:S(2)}, u32[]{:S(2)}) collective-permute-start(bf16[128,128]{1,0:T(8,128)(2,1)S(1)} %reduce_sum.75), channel_id=1, source_target_pairs={{0,64},{64,0},{1,65},{65,1},{2,66},{66,2},{3,67},{67,3},{4,68},{68... | collective-permute-start | bytes 98312 | tf_op jit(solution)/shard_map/ppermute | solution.py:14

commit v2 on v1

v2 whole, which is shorter than its diff:
```python
import jax
import jax.numpy as jnp
from jax import lax
from jax.sharding import PartitionSpec as P


def from_partner(block, axis, apart):
    count = lax.axis_size(axis)
    route = []
    for low in range(count):
        high = low | 1 << apart
        if high != low and high < count:
            route += [(low, high), (high, low)]
    return lax.ppermute(block, axis, route)


def step(innov, pred, obs_weight, owner, counts, neighbours, loc_weight, ensemble):
    tiles = lax.axis_size("tile")
    members = pred.shape[2]
    obs_rows = pred.shape[1]
    blocks = owner.shape[0]
    block_rows = obs_rows // blocks
    slot_count = max(2, 2 * blocks // tiles)
    block_ids = jnp.arange(blocks, dtype=jnp.int32)
    live = (block_ids < counts[0]).astype(jnp.float32)
    row_scale = obs_weight * jnp.repeat(live, block_rows)
    zed = (pred[0].astype(jnp.float32) * row_scale[:, None]).astype(jnp.bfloat16)
    unn = (innov[0].astype(jnp.float32) * row_scale[:, None]).astype(jnp.bfloat16)
    partner_zed = from_partner(zed, "half", 0)

    dest = owner[:, 0]
    same = (dest[None, :] == dest[:, None]) & (block_ids[None, :] < block_ids[:, None])
    rank = jnp.sum(same.astype(jnp.int32), axis=1)
    position = dest * slot_count + rank
    slot_ids = jnp.arange(tiles * slot_count, dtype=jnp.int32)
    hit = position[None, :] == slot_ids[:, None]
    source = jnp.sum(hit.astype(jnp.int32) * block_ids[None, :], axis=1)
    filled = jnp.any(hit, axis=1)

    def slots(rows):
        got = jnp.where(filled[:, None, None], rows.reshape(blocks, block_rows, members)[source], jnp.zeros((), rows.dtype))
        return got.reshape(tiles, slot_count * block_rows, members)

    dims = (((1,), (1,)), ((0,), (0,)))
    eye = jnp.eye(members, dtype=jnp.float32)
    own_zed = slots(zed)
    gram_part = lax.dot_general(own_zed, own_zed, dims, preferred_element_type=jnp.float32)
    gram = jnp.sum(lax.all_to_all(gram_part, "tile", 0, 0, tiled=True), axis=0)
    factor = jnp.linalg.cholesky((members - 1.0) * eye + gram)
    partner_factor = from_partner(factor, "half", 0)
    ens_f = ensemble[0].astype(jnp.float32)
    center = jnp.mean(ens_f, axis=1, keepdims=True)
    anomalies = (ens_f - center).astype(jnp.bfloat16)
    anomalies, partner_zed, partner_factor = lax.optimization_barrier((anomalies, partner_zed, partner_factor))
    partner_anom = from_partner(anomalies, "half", 0)

    other_zed = slots(partner_zed)
    own_unn = slots(unn)
    cross_part = lax.dot_general(other_zed, own_unn, dims, preferred_element_type=jnp.float32)
    cross = jnp.sum(lax.all_to_all(cross_part, "tile", 0, 0, tiled=True), axis=0)
    weights = jax.scipy.linalg.cho_solve((partner_factor, True), cross)
    tile_ids = jnp.arange(tiles, dtype=jnp.int32)
    loc_row = jnp.sum(
        loc_weight[0][:, None] * (neighbours[0][:, None] == tile_ids[None, :]).astype(jnp.float32),
        axis=0,
    )
    reach = loc_row[:, None, None] * weights[None, :, :]
    spread = jnp.sum(lax.all_to_all(reach, "tile", 0, 0, tiled=True), axis=0).astype(jnp.bfloat16)
    incr = jnp.dot(partner_anom, spread, preferred_element_type=jnp.float32).astype(jnp.bfloat16)
    analysis = (ens_f + incr.astype(jnp.float32)).astype(jnp.bfloat16)
    return analysis[None]


def solution(mesh):
    return jax.shard_map(
        step,
        mesh=mesh,
        in_specs=(
            P("half", "tile", None),
            P("half", "tile", None),
            P("tile"),
            P("tile", None),
            P("tile"),
            P("tile", None),
            P("tile", None),
            P("half", "tile", None),
        ),
        out_specs=P("half", "tile", None),
        check_vma=False,
    )
```

time: 406 us -> 434 us (1.069)
  other arithmetic: 62.8 us -> 74.6 us
  local copies, waits for them, and re-layouts: 21.6 us -> 32.2 us
  waiting for transfers between devices: 133 us -> 138 us
    all_to_all x1, waiting for transfers between devices: 22.8 us -> 39.1 us  [step(): lax.all_to_all(cross_part, 'tile', 0, 0, tiled=True)]
    ppermute x3, waiting for transfers between devices: 69.1 us -> 57.9 us  [from_partner(): return lax.ppermute(block, axis, route)]
    gather x2 -> x3, local copies, waits for them, and re-layouts: 21.2 us -> 31.9 us  [slots(): rows.reshape(blocks, block_rows, members)[source]]
    select_n x2 -> x4, other arithmetic: 11.9 us -> 20.4 us  [the longest x2 19.7 us: slots(): jnp.where(filled[:, None, None], rows.reshape(blocks, block_rows, members...]
  transfers between devices with their start and end apart: 5 -> 5, of which waited for: 4 -> 3; matrix products, arithmetic and copies ran while one was open for 16% -> 13% of each run, Pallas kernels for 0% -> 0%
where the time goes in v2:
time: 434 us; the launch traced here: 431 us
  waiting for transfers between devices  138 us (32%)
  blocking collectives  130 us (30%)
  other arithmetic  74.6 us (17%)
  local copies, waits for them, and re-layouts  32.2 us (7%)
  matrix products  27.6 us (6%)
  starting transfers between devices  27.5 us (6%)
    all_to_all x1, blocking collectives, step(): lax.all_to_all(reach, 'tile', 0, 0, tiled=True)  130 us
    ppermute x3, waiting for transfers between devices, from_partner(): return lax.ppermute(block, axis, route)  57.9 us
    all_to_all x1, waiting for transfers between devices, step(): gram = jnp.sum(lax.all_to_all(gram_part, 'tile', 0, 0, tiled=True), axis=0)  41 us
    all_to_all x1, waiting for transfers between devices, step(): lax.all_to_all(cross_part, 'tile', 0, 0, tiled=True)  39.1 us
    gather x3, local copies, waits for them, and re-layouts, slots(): rows.reshape(blocks, block_rows, members)[source]  31.9 us
    select_n x2, other arithmetic, slots(): jnp.where(filled[:, None, None], rows.reshape(blocks, block_rows, members...  19.7 us
    another operation x3, other arithmetic, step(): factor = jnp.linalg.cholesky((members - 1.0) * eye + gram)  12.4 us
    dot_general x1, matrix products, step(): lax.dot_general(own_zed, own_zed, dims, preferred_element_type=jnp.float32)  10.2 us
  transfers between devices with their start and end apart: 5, of which 3 were waited for; matrix products, arithmetic and copies ran while one was open for 13% of the time, Pallas kernels for 0%

profile of v2, /device:TPU:0, one launch (start us, length us, event | category | flops | bytes accessed | tf_op | source)
XLA Modules:
  0.0 430.6 jit_solution(17580606998686279994)
XLA Ops:
  0.0 0.9 convert_reduce_fusion.1
  0.9 0.7 multiply_add_fusion
  2.8 0.9 bitcast_multiply_fusion.1
  3.7 8.6 %fusion.6 = (bf16[128,128,128]{2,1,0:T(8,128)(2,1)}, bf16[128,128,128]{2,1,0:T(8,128)(2,1)}) fusion(bf16[128,128,128]{2,1,0:T(8,128)(2,1)} %bitcast.67, f32[128,128]{1,0:T(8,128)S(1)} %bitcast.68, bf16[128,128,128]{2,1,0:T(8,128)(2,1)} %bitcast.66), kind=kLoop, calls=%fused_computation.13 | loop fusion | flops 12582912 | bytes 16842752 | tf_op jit(solution)/shard_map/convert_element_type | solution.py:28
  12.3 10.6 %gather_fusion = bf16[256,128,128]{2,1,0:T(8,128)(2,1)} fusion(bf16[128,128,128]{2,1,0:T(8,128)(2,1)} %get-tuple-element.12, s32[1024]{0:T(1024)S(1)} %pad_clamp_fusion), kind=kCustom, calls=%fused_computation | custom fusion | bytes 16778240 | tf_op jit(solution)/shard_map/gather | solution.py:41
  22.9 7.8 %bitcast_select_fusion.2 = bf16[64,512,128]{2,1,0:T(8,128)(2,1)} fusion(pred[64,512]{1,0:T(8,128)(4,1)S(1)} %bitcast.69, bf16[64,512,128]{2,1,0:T(8,128)(2,1)} %bitcast.65), kind=kLoop, calls=%fused_computation.16 | loop fusion | flops 4194304 | bytes 16809984 | tf_op jit(solution)/shard_map/jit(_where)/select_n | solution.py:41
  30.7 10.2 %fusion.17 = f32[64,128,128]{2,1,0:T(8,128)} fusion(bf16[64,512,128]{2,1,0:T(8,128)(2,1)} %bitcast_select_fusion.2), kind=kOutput, calls=%fused_computation.51 | convolution fusion | flops 1073741824 | bytes 12582912 | tf_op jit(solution)/shard_map/dot_general | solution.py:47
  40.9 10.2 %all-to-all-start = ((f32[64,128,128]{2,1,0:T(8,128)}), f32[64,128,128]{2,1,0:T(8,128)}, u32[]{:S(2)}, u32[]{:S(2)}) async-start(f32[64,128,128]{2,1,0:T(8,128)} %fusion.17), calls=%async_computation | async-start | bytes 8388608 | tf_op jit(solution)/shard_map/all_to_all | solution.py:48
  51.1 6.0 %fusion.7 = bf16[16384,128]{1,0:T(8,128)(2,1)} fusion(f32[16384]{0:T(1024)S(1)} %bitcast_multiply_fusion.1, bf16[1,16384,128]{2,1,0:T(8,128)(2,1)} %param.9), kind=kLoop, calls=%fused_computation.18 | loop fusion | flops 6291456 | bytes 8454144 | tf_op jit(solution)/shard_map/convert_element_type | solution.py:27
  57.1 2.9 collective-permute-start
  60.0 1.3 convert_reduce_fusion
  61.3 41.0 %all-to-all-done = f32[64,128,128]{2,1,0:T(8,128)} async-done(((f32[64,128,128]{2,1,0:T(8,128)}), f32[64,128,128]{2,1,0:T(8,128)}, u32[]{:S(2)}, u32[]{:S(2)}) %all-to-all-start) | async-done | bytes 4194336 | tf_op jit(solution)/shard_map/all_to_all | solution.py:48
  102.3 2.4 reduce_sum.71
  104.8 11.7 %cholesky.19 = f32[128,128]{1,0:T(8,128)S(1)} custom-call(f32[128,128]{1,0:T(8,128)S(1)} %fusion.14), custom_call_target="Cholesky" | custom-call | tf_op jit(solution)/shard_map/jit(cholesky)/cholesky | solution.py:49
  116.6 0.6 compare_reduce_fusion
  117.2 0.7 select_select_fusion
  117.9 3.0 collective-permute-start.1
  120.9 5.8 %fusion.5 = bf16[16384,128]{1,0:T(8,128)(2,1)} fusion(bf16[1,16384,128]{2,1,0:T(8,128)(2,1)} %param.15, f32[16384]{0:T(1024)S(1)} %broadcast_multiply_fusion.1), kind=kLoop, calls=%fused_computation.11 | loop fusion | flops 6291456 | bytes 8454144 | tf_op jit(solution)/shard_map/convert_element_type | solution.py:53
  126.7 10.6 %gather_fusion.2 = bf16[256,128,128]{2,1,0:T(8,128)(2,1)} fusion(bf16[128,128,128]{2,1,0:T(8,128)(2,1)} %get-tuple-element.11, s32[1024]{0:T(1024)S(1)} %pad_clamp_fusion), kind=kCustom, calls=%fused_computation.2 | custom fusion | bytes 16778240 | tf_op jit(solution)/shard_map/gather | solution.py:41
  137.3 57.9 %collective-permute-done.1 = f32[128,128]{1,0:T(8,128)S(1)} collective-permute-done((f32[128,128]{1,0:T(8,128)S(1)}, f32[128,128]{1,0:T(8,128)S(1)}, u32[]{:S(2)}, u32[]{:S(2)}) %collective-permute-start.1) | collective-permute-done | bytes 65568 | tf_op jit(solution)/shard_map/ppermute | solution.py:14
  195.2 10.6 %gather_fusion.1 = bf16[256,128,128]{2,1,0:T(8,128)(2,1)} fusion(bf16[128,128,128]{2,1,0:T(8,128)(2,1)} %bitcast.15, s32[1024]{0:T(1024)S(1)} %pad_clamp_fusion), kind=kCustom, calls=%fused_computation.1 | custom fusion | bytes 16778240 | tf_op jit(solution)/shard_map/gather | solution.py:41
  205.8 11.9 %bitcast_select_fusion = (bf16[64,512,128]{2,1,0:T(8,128)(2,1)}, bf16[64,512,128]{2,1,0:T(8,128)(2,1)}) fusion(pred[64,512]{1,0:T(8,128)(4,1)S(1)} %bitcast.70, bf16[64,512,128]{2,1,0:T(8,128)(2,1)} %bitcast.63, bf16[64,512,128]{2,1,0:T(8,128)(2,1)} %bitcast.64), kind=kLoop, calls=%fused_computation.14 | loop fusion | flops 8388608 | bytes 33587200 | tf_op jit(solution)/shard_map/jit(_where)/select_n | solution.py:41
  217.7 10.2 %fusion.18 = f32[64,128,128]{2,1,0:T(8,128)} fusion(bf16[64,512,128]{2,1,0:T(8,128)(2,1)} %get-tuple-element.14, bf16[64,512,128]{2,1,0:T(8,128)(2,1)} %get-tuple-element.13), kind=kOutput, calls=%fused_computation.52 | convolution fusion | flops 1073741824 | bytes 20971520 | tf_op jit(solution)/shard_map/dot_general | solution.py:59
  227.9 9.3 %all-to-all-start.1 = ((f32[64,128,128]{2,1,0:T(8,128)}), f32[64,128,128]{2,1,0:T(8,128)}, u32[]{:S(2)}, u32[]{:S(2)}) async-start(f32[64,128,128]{2,1,0:T(8,128)} %fusion.18), calls=%async_computation.1 | async-start | bytes 8388608 | tf_op jit(solution)/shard_map/all_to_all | solution.py:60
  237.3 9.8 %custom-call.10 = f32[1,128,128]{1,2,0:T(8,128)S(1)} custom-call(f32[1,128,128]{2,1,0:T(8,128)S(1)} %select_bitcast_fusion), custom_call_target="InvertDiagBlocksLowerTriangular" | custom-call | tf_op jit(solution)/shard_map/jit(_cho_solve)/triangular_solve | solution.py:61
  247.1 2.1 collective-permute-start.2
  249.3 39.1 %all-to-all-done.1 = f32[64,128,128]{2,1,0:T(8,128)} async-done(((f32[64,128,128]{2,1,0:T(8,128)}), f32[64,128,128]{2,1,0:T(8,128)}, u32[]{:S(2)}, u32[]{:S(2)}) %all-to-all-start.1) | async-done | bytes 4194336 | tf_op jit(solution)/shard_map/all_to_all | solution.py:60
  288.4 2.4 reduce_sum.74
  291.3 0.3 broadcast_multiply_fusion
  291.6 129.8 %all_to_all.15 = f32[64,128,128]{2,1,0:T(8,128)} all-to-all(f32[64,128,128]{2,1,0:T(8,128)S(1)} %broadcast_multiply_fusion), channel_id=1, replica_groups=mesh['half'=2,'tile'=64] {'tile'}, dimensions={0} | all-to-all | bytes 8388608 | tf_op jit(solution)/shard_map/all_to_all | solution.py:68
  421.4 2.4 reduce_sum.75
  423.8 6.7 %fusion.3 = bf16[1,16384,128]{2,1,0:T(8,128)(2,1)} fusion(bf16[16384,128]{1,0:T(8,128)(2,1)} %collective-permute-done.2, bf16[1,16384,128]{2,1,0:T(8,128)(2,1)} %param.15, bf16[128,128]{1,0:T(8,128)(2,1)S(1)} %reduce_sum.75), kind=kOutput, calls=%fused_computation.7 | convolution fusion | flops 547356672 | bytes 12615680 | tf_op jit(solution)/shard_map/dot_general | solution.py:69
  (24 shorter events, 1.3 us)
Async XLA Ops:
  40.9 61.4 %all-to-all-start = ((f32[64,128,128]{2,1,0:T(8,128)}), f32[64,128,128]{2,1,0:T(8,128)}, u32[]{:S(2)}, u32[]{:S(2)}) async-start(f32[64,128,128]{2,1,0:T(8,128)} %fusion.17), calls=%async_computation | async-start | bytes 8388608 | tf_op jit(solution)/shard_map/all_to_all | solution.py:48
  51.1 8.9 %copy-start = (bf16[1,16384,128]{2,1,0:T(8,128)(2,1)S(1)}, bf16[1,16384,128]{2,1,0:T(8,128)(2,1)}, u32[]{:S(2)}) copy-start(bf16[1,16384,128]{2,1,0:T(8,128)(2,1)} %param.15) | copy-start | bytes 12582916
  57.1 138.1 %collective-permute-start = (bf16[16384,128]{1,0:T(8,128)(2,1)}, bf16[16384,128]{1,0:T(8,128)(2,1)}, u32[]{:S(2)}, u32[]{:S(2)}) collective-permute-start(bf16[16384,128]{1,0:T(8,128)(2,1)} %fusion.7), channel_id=1, source_target_pairs={{0,64},{64,0},{1,65},{65,1},{2,66},{66,2},{3,67},{67,3},{4,68},{68... | collective-permute-start | bytes 12582920 | tf_op jit(solution)/shard_map/ppermute | solution.py:14
  117.9 77.3 %collective-permute-start.1 = (f32[128,128]{1,0:T(8,128)S(1)}, f32[128,128]{1,0:T(8,128)S(1)}, u32[]{:S(2)}, u32[]{:S(2)}) collective-permute-start(f32[128,128]{1,0:T(8,128)S(1)} %select_select_fusion), channel_id=1, source_target_pairs={{0,64},{64,0},{1,65},{65,1},{2,66},{66,2},{3,67},{67,3},{4,68},{68... | collective-permute-start | bytes 196616 | tf_op jit(solution)/shard_map/ppermute | solution.py:14
  227.9 9.3 %copy-start.1 = (f32[1,9]{1,0:T(1,128)S(1)}, f32[1,9]{1,0:T(1,128)}, u32[]{:S(2)}) copy-start(f32[1,9]{1,0:T(1,128)} %param.14) | copy-start | bytes 112
  227.9 9.3 %copy-start.2 = (s32[1,9]{1,0:T(1,128)S(1)}, s32[1,9]{1,0:T(1,128)}, u32[]{:S(2)}) copy-start(s32[1,9]{1,0:T(1,128)} %param.13) | copy-start | bytes 112
  227.9 60.5 %all-to-all-start.1 = ((f32[64,128,128]{2,1,0:T(8,128)}), f32[64,128,128]{2,1,0:T(8,128)}, u32[]{:S(2)}, u32[]{:S(2)}) async-start(f32[64,128,128]{2,1,0:T(8,128)} %fusion.18), calls=%async_computation.1 | async-start | bytes 8388608 | tf_op jit(solution)/shard_map/all_to_all | solution.py:60
  247.1 176.7 %collective-permute-start.2 = (bf16[16384,128]{1,0:T(8,128)(2,1)}, bf16[16384,128]{1,0:T(8,128)(2,1)}, u32[]{:S(2)}, u32[]{:S(2)}) collective-permute-start(bf16[16384,128]{1,0:T(8,128)(2,1)} %fusion.5), channel_id=1, source_target_pairs={{0,64},{64,0},{1,65},{65,1},{2,66},{66,2},{3,67},{67,3},{4,68},{68... | collective-permute-start | bytes 12582920 | tf_op jit(solution)/shard_map/ppermute | solution.py:14
